TPU v7x, 256 devices: a whole 4x4x8 slice. The times are simulated.
256 devices in a mesh: dp: 16 (over y, z_hi, core), tensor: 16 (over z_lo, x).
Axes of the slice: x: 4, y: 4, z: 8 (z_hi: 2, z_lo: 4; z = z_hi * 4 + z_lo), core: 2. Of those that a mesh axis runs over, the one named last changes fastest.
Arguments:
- token_ids: int32 [4096], P('dp'), may hold values from 0 to 128255
- attn_heads: bfloat16 [4096, 8192], P('dp', 'tensor'), may hold values from -6 to 6
- out_proj: bfloat16 [8192, 8192], P('tensor'), may hold values from -0.0625 to 0.0625
- residual: bfloat16 [4096, 8192], P(('dp', 'tensor')), may hold values from -6 to 6
- norm_gain: float32 [8192], replicated, may hold values from 0.5 to 1.5
- twist_in: bfloat16 [8192, 8192], P('dp', 'tensor'), may hold values from -0.0625 to 0.0625
- twist_out: float32 [8192], P('tensor'), may hold values from -0.26516503 to 0.26516503
- token_bias: float32 [128256], replicated, may hold values from -4 to 262
- toxicity: int32 [16], P('dp'), may hold values from 1 to 4
- prompt_len: int32 [16], P('dp'), may hold values from 1 to 128
Outputs:
- twist_vals: float32 [4096], P('dp')
- grad_in: float32 [8192, 8192], P('dp', 'tensor')
- grad_out: float32 [8192], P('tensor')
- grad_bias: float32 [128256], P('dp')
All inputs are finite; a program needn't handle non-finite values.
Results may differ from a plain program's by a relative error of at most 0.033.
Values may be sent and summed in bfloat16 or wider, within the bound.
No kernel may reach another device: no remote copies, remote signals or barrier semaphores. Data moves between devices by JAX's collectives and lax.ppermute only.
A program may use at most 128 MiB of HBM per device.

v0:
```python
import jax
import jax.numpy as jnp
from jax import lax
from jax.sharding import PartitionSpec as P


def merged_2(value, axis, join):
    pieces = jax.tree.map(lambda part: lax.all_gather(part, axis), value)
    head = jax.tree.map(lambda part: part[0], pieces)
    tail = jax.tree.map(lambda part: part[1:], pieces)
    total, _ = lax.scan(lambda total, share: (join(total, share), None), head, tail)
    return total


def normalize(hidden, norm_gain):
    values = hidden.astype(jnp.float32)
    scaled = lax.rsqrt(jnp.mean(values * values, axis=-1, keepdims=True) + 1e-05)
    return (values * scaled * norm_gain[None, :]).astype(jnp.bfloat16)


def combine(earlier, later):
    high_one, sum_one, lab_one = earlier
    high_two, sum_two, lab_two = later
    highest = jnp.maximum(high_one, high_two)
    merged = sum_one * jnp.exp(high_one - highest) + sum_two * jnp.exp(high_two - highest)
    return (highest, merged, lab_one + lab_two)


def local(
    token_ids,
    attn_heads,
    out_proj,
    residual,
    norm_gain,
    twist_in,
    twist_out,
    token_bias,
    toxicity,
    prompt_len,
):
    seq_len = attn_heads.shape[0]
    vocab_size = token_bias.shape[0]
    partial_sum = jnp.dot(attn_heads, out_proj, preferred_element_type=jnp.float32)
    summed = lax.psum(partial_sum.astype(jnp.bfloat16), "tensor").astype(jnp.float32)
    resid_all = lax.all_gather(residual, "tensor", axis=0, tiled=True)
    hidden = (resid_all.astype(jnp.float32) + summed).astype(jnp.bfloat16)
    normed = normalize(hidden, norm_gain)
    columns = normed
    pre_act = jnp.dot(
        columns,
        lax.all_gather(twist_in, "dp", axis=0, tiled=True),
        preferred_element_type=jnp.float32,
    )
    active = jax.nn.silu(pre_act)
    partial_psi = jnp.dot(active, twist_out, precision=lax.Precision.HIGHEST)
    twist_vals = lax.psum(partial_psi, "tensor") + token_bias[token_ids]
    live = jnp.arange(seq_len) >= prompt_len[0]
    live_float = live.astype(jnp.float32)
    levels = toxicity[0].astype(jnp.float32) * live_float
    local_high = jnp.where(live, twist_vals, -1e30)
    highest, totals, lab_sum = merged_2((local_high, live_float, levels), "dp", combine)
    expo = jnp.where(live, jnp.exp(jnp.where(live, twist_vals - highest, -80.0)), 0.0)
    weights = (expo / jnp.maximum(totals, 1.0) - levels / jnp.maximum(lab_sum, 1.0)) / seq_len
    grad_out = lax.psum(jnp.dot(weights, active, precision=lax.Precision.HIGHEST), "dp")
    local_bias = jnp.zeros((vocab_size,), jnp.float32).at[token_ids].add(weights)
    grad_bias = lax.psum_scatter(
        local_bias.astype(jnp.bfloat16), "dp", scatter_dimension=0, tiled=True
    ).astype(jnp.float32)
    sigma = jax.nn.sigmoid(pre_act)
    d_pre = (
        weights[:, None] * twist_out[None, :] * sigma * (1.0 + pre_act * (1.0 - sigma))
    ).astype(jnp.bfloat16)
    contract = (((0,), (0,)), ((), ()))
    columns = normed
    grad_in = lax.psum_scatter(
        lax.dot_general(columns, d_pre, contract, preferred_element_type=jnp.float32).astype(
            jnp.bfloat16
        ),
        "dp",
        scatter_dimension=0,
        tiled=True,
    ).astype(jnp.float32)
    return (twist_vals, grad_in, grad_out, grad_bias)


def solution(mesh):
    placed = (
        P("dp"),
        P("dp", "tensor"),
        P("tensor", None),
        P(("dp", "tensor"), None),
        P(),
        P("dp", "tensor"),
        P("tensor"),
        P(),
        P("dp"),
        P("dp"),
    )
    return jax.shard_map(
        local,
        mesh=mesh,
        in_specs=placed,
        out_specs=(P("dp"), P("dp", "tensor"), P("tensor"), P("dp")),
        check_vma=False,
    )
```

profile of v0, /device:TPU:2, one launch (start us, length us, event | category | flops | bytes accessed | tf_op | source)
XLA Modules:
  0.0 797.6 jit_solution(13153336247750633944)
XLA Ops:
  7.2 0.0 copy-start
  7.2 0.0 copy-start.2
  7.2 0.0 all-reduce.4.cloned.1.call-start
  7.2 7.8 convolution_convert_fusion.1
  15.1 0.0 copy-start.3
  15.1 0.0 all-reduce.4.cloned.1.call-update
  15.1 0.0 all-gather.7.cloned.1.call-start
  15.1 0.7 all-gather.7.cloned.1.call-update
  15.8 0.0 all-gather.9.cloned.1.call-start
  15.9 0.7 all-gather.9.cloned.1.call-update
  16.6 0.0 all-reduce.6.cloned.1.call-start
  17.9 33.4 %all-gather.3 = f32[16,1,256]{2,1,0:T(1,128)S(1)} all-gather(f32[1,1,256]{2,1,0:T(1,128)S(1)} %fusion.13), channel_id=1, replica_groups=mesh['dp'=16,'tensor'=16] {'dp'}, dimensions={0}, use_global_device_ids=true | all-gather | bytes 17408 | tf_op jit(solution)/shard_map/all_gather | solution.py:8
  51.4 24.1 %all-gather.2 = f32[16,1,256]{2,1,0:T(1,128)S(1)} all-gather(f32[1,1,256]{2,1,0:T(1,128)S(1)} %fusion.14), channel_id=1, replica_groups=mesh['dp'=16,'tensor'=16] {'dp'}, dimensions={0}, use_global_device_ids=true | all-gather | bytes 17408 | tf_op jit(solution)/shard_map/all_gather | solution.py:8
  75.5 0.0 copy-done.2
  75.5 0.0 copy-done
  75.5 1.7 gather_fusion
  77.3 118.5 %all-reduce.4.cloned.1.call-done = bf16[256,8192]{1,0:T(8,128)(2,1)} async-done(((bf16[256,8192]{1,0:T(8,128)(2,1)}), bf16[256,8192]{1,0:T(8,128)(2,1)}) %all-reduce.4.cloned.1.call-update) | async-done | bytes 4194320 | tf_op jit(solution)/shard_map/psum | solution.py:44
  195.8 87.7 %all-gather.7.cloned.1.call-done = bf16[256,8192]{1,0:T(8,128)(2,1)} async-done(((bf16[16,8192]{1,0:T(8,128)(2,1)}), bf16[256,8192]{1,0:T(8,128)(2,1)}) %all-gather.7.cloned.1.call-update) | async-done | bytes 4194320 | tf_op jit(solution)/shard_map/all_gather | solution.py:45
  283.5 4.9 fusion
  288.4 0.0 copy-start.4
  288.5 104.6 %all-gather.9.cloned.1.call-done = bf16[8192,512]{1,0:T(8,128)(2,1)} async-done(((bf16[512,512]{1,0:T(8,128)(2,1)}), bf16[8192,512]{1,0:T(8,128)(2,1)}) %all-gather.9.cloned.1.call-update) | async-done | bytes 8388624 | tf_op jit(solution)/shard_map/all_gather | solution.py:51
  393.1 0.0 copy-done.3
  393.1 8.2 %fusion.20 = f32[256,512]{1,0:T(8,128)S(1)} fusion(bf16[8192,512]{1,0:T(8,128)(2,1)} %all-gather.9.cloned.1.call-done, f32[8192]{0:T(1024)S(1)} %copy-done.3, f32[256]{0:T(256)S(1)} %add_rsqrt_fusion, bf16[256,8192]{1,0:T(8,128)(2,1)} %all-reduce.4.cloned.1.call-done, bf16[256,8192]{1,0:T(8,128)(2,1)} %all-gather.7.cloned.1.call-done), kind=kOutput, calls=%fused_computation.41 | convolution fusion | flops 2164260864 | bytes 17335296 | tf_op jit(solution)/shard_map/dot_general | solution.py:49
  401.3 0.0 copy-done.4
  401.4 0.6 fusion.11
  402.0 38.4 %psum.22 = f32[256]{0:T(256)S(1)} all-reduce(f32[256]{0:T(256)S(1)} %bitcast.53), channel_id=1, replica_groups=mesh['dp'=16,'tensor'=16] {'tensor'}, use_global_device_ids=true, to_apply=%region_2.3 | all-reduce | flops 256 | bytes 2048 | tf_op jit(solution)/shard_map/psum | solution.py:56
  440.3 0.0 copy-start.1
  440.3 23.8 %all-gather.1 = f32[16,1,256]{2,1,0:T(1,128)S(1)} all-gather(f32[1,1,256]{2,1,0:T(1,128)S(1)} %bitcast.51), channel_id=2, replica_groups=mesh['dp'=16,'tensor'=16] {'dp'}, dimensions={0}, use_global_device_ids=true | all-gather | bytes 17408 | tf_op jit(solution)/shard_map/all_gather | solution.py:8
  464.1 1.3 while.14
  465.4 2.1 scatter_custom_fusion
  467.5 0.7 convert_element_type.61
  468.2 0.0 all-reduce.6.cloned.1.call-update
  468.3 0.2 reduce-scatter.2.cloned.1.call-start
  468.5 10.1 %convolution_convert_fusion = bf16[8192,512]{1,0:T(8,128)(2,1)} fusion(f32[256,512]{1,0:T(8,128)S(1)} %fusion.20, f32[512]{0:T(512)S(1)} %copy-done.4, f32[256]{0:T(256)S(1)} %subtract_multiply_fusion, f32[8192]{0:T(1024)S(1)} %copy-done.3, f32[256]{0:T(256)S(1)} %add_rsqrt_fusion, bf16[256,8192]{1,0:T(8,128)(2,1)} %all-reduce.4.cloned.1.call-done, ...), kind=kOutput, calls=%fused_computation.6 | convolution fusion | flops 2169765888 | bytes 17338368 | tf_op jit(solution)/shard_map/dot_general | solution.py:76
  478.6 0.0 copy-done.1
  478.6 0.0 copy-start.5
  478.6 0.0 reduce-scatter.2.cloned.1.call-update
  478.6 0.6 copy-done.5
  479.2 0.6 dynamic-slice
  480.5 0.5 fusion.9
  480.9 49.3 %psum.23 = f32[512]{0:T(512)} all-reduce(f32[512]{0:T(512)S(1)} %bitcast.52), channel_id=1, replica_groups=mesh['dp'=16,'tensor'=16] {'dp'}, use_global_device_ids=true, to_apply=%region_6.7 | all-reduce | flops 512 | bytes 4096 | tf_op jit(solution)/shard_map/psum | solution.py:64
  530.2 113.1 %all-reduce.6.cloned.1.call-done = bf16[128256]{0:T(1024)(128)(2,1)} async-done(((bf16[128256]{0:T(1024)(128)(2,1)}), bf16[128256]{0:T(1024)(128)(2,1)}) %all-reduce.6.cloned.1.call-update) | async-done | bytes 256528
  643.3 1.4 dynamic-slice_convert_fusion
  644.7 144.2 %reduce-scatter.2.cloned.1.call-done = bf16[512,512]{1,0:T(8,128)(2,1)} async-done(((bf16[8192,512]{1,0:T(8,128)(2,1)}), bf16[512,512]{1,0:T(8,128)(2,1)}) %reduce-scatter.2.cloned.1.call-update) | async-done | bytes 524304 | tf_op jit(solution)/shard_map/reduce_scatter | solution.py:75
  788.9 2.1 convert_element_type.60
  (76 shorter events, 0.9 us)
Async XLA Ops:
  7.2 68.4 %copy-start = (f32[128256]{0:T(1024)S(1)}, f32[128256]{0:T(1024)}, u32[]{:S(2)}) copy-start(f32[128256]{0:T(1024)} %param.19) | copy-start | bytes 1539076
  7.2 68.3 %copy-start.2 = (s32[256]{0:T(256)S(1)}, s32[256]{0:T(256)}, u32[]{:S(2)}) copy-start(s32[256]{0:T(256)} %param.12) | copy-start | bytes 3076
  7.2 188.6 %all-reduce.4.cloned.1.call-start = ((), (), s32[]{:S(2)}) async-start(), calls=%async_computation.2 | async-start | bytes 8388608 | tf_op jit(solution)/shard_map/psum | solution.py:44
  15.1 378.0 %copy-start.3 = (f32[8192]{0:T(1024)S(1)}, f32[8192]{0:T(1024)}, u32[]{:S(2)}) copy-start(f32[8192]{0:T(1024)} %param.16) | copy-start | bytes 98308
  15.1 268.4 %all-gather.7.cloned.1.call-start = ((), (), s32[]{:S(2)}) async-start(), calls=%async_computation.1 | async-start | bytes 4456448 | tf_op jit(solution)/shard_map/all_gather | solution.py:45
  15.8 377.3 %all-gather.9.cloned.1.call-start = ((), (), s32[]{:S(2)}) async-start(), calls=%async_computation.3 | async-start | bytes 8912896 | tf_op jit(solution)/shard_map/all_gather | solution.py:51
  16.6 626.7 %all-reduce.6.cloned.1.call-start = ((), (), s32[]{:S(2)}) async-start(), calls=%async_computation.5 | async-start | bytes 516096
  288.4 112.9 %copy-start.4 = (f32[512]{0:T(512)S(1)}, f32[512]{0:T(512)}, u32[]{:S(2)}) copy-start(f32[512]{0:T(512)} %param.18) | copy-start | bytes 6148
  440.3 38.2 %copy-start.1 = (f32[256]{0:T(256)}, f32[256]{0:T(256)S(1)}, u32[]{:S(2)}) copy-start(f32[256]{0:T(256)S(1)} %get-tuple-element.63) | copy-start | bytes 3076
  468.3 320.7 %reduce-scatter.2.cloned.1.call-start = ((), (), s32[]{:S(2)}) async-start(), calls=%async_computation.4 | async-start | bytes 8912896 | tf_op jit(solution)/shard_map/reduce_scatter | solution.py:75
  478.6 0.7 copy-start.5
Sparse Core Ops, SparseCore 0:
  15.2 180.5 all-reduce.3
  197.6 85.8 all-gather.6
  286.2 106.8 all-gather.8
  468.4 174.8 all-reduce.5
  647.8 141.1 reduce-scatter.1
where the time goes:
time: 798 us
  waiting for transfers between devices  570 us (71%)
  blocking collectives  169 us (21%)
  matrix products  27.2 us (3%)
  between operations  15.9 us (2%)
  other arithmetic  11.8 us (1%)
    reduce_scatter x1, waiting for transfers between devices, local(): lax.psum_scatter(lax.dot_general(columns, d_pre, contract, preferred_elem...  144 us
    psum x1, waiting for transfers between devices, local(): lax.psum(partial_sum.astype(jnp.bfloat16), 'tensor').astype(jnp.float32)  119 us
    unnamed x6, waiting for transfers between devices  115 us
    all_gather x1, waiting for transfers between devices, local(): lax.all_gather(twist_in, 'dp', axis=0, tiled=True)  105 us
    all_gather x1, waiting for transfers between devices, local(): resid_all = lax.all_gather(residual, 'tensor', axis=0, tiled=True)  87.7 us
    all_gather x3, blocking collectives, merged_2(): pieces = jax.tree.map(lambda part: lax.all_gather(part, axis), value)  81.4 us
    psum x1, blocking collectives, local(): lax.psum(jnp.dot(weights, active, precision=lax.Precision.HIGHEST), 'dp')  49.3 us
    psum x1, blocking collectives, local(): twist_vals = lax.psum(partial_psi, 'tensor') + token_bias[token_ids]  38.4 us
  transfers between devices with their start and end apart: 5, of which 5 were waited for; matrix products, arithmetic and copies ran while one was open for 2% of the time, Pallas kernels for 0%

commit v1 on v0

--- a/solution.py
+++ b/solution.py
@@ -41,7 +41,9 @@
     seq_len = attn_heads.shape[0]
     vocab_size = token_bias.shape[0]
     partial_sum = jnp.dot(attn_heads, out_proj, preferred_element_type=jnp.float32)
-    summed = lax.psum(partial_sum.astype(jnp.bfloat16), "tensor").astype(jnp.float32)
+    summed = jnp.sum(lax.all_gather(partial_sum.astype(jnp.bfloat16), "tensor"), axis=0).astype(
+        jnp.float32
+    )
     resid_all = lax.all_gather(residual, "tensor", axis=0, tiled=True)
     hidden = (resid_all.astype(jnp.float32) + summed).astype(jnp.bfloat16)
     normed = normalize(hidden, norm_gain)

time: 798 us -> 1310 us (1.64)
  waiting for transfers between devices: 570 us -> 1060 us
  other arithmetic: 11.8 us -> 35.6 us
    all_gather x0 -> x1, waiting for transfers between devices: none -> 629 us  [local(): lax.all_gather(partial_sum.astype(jnp.bfloat16), 'tensor')]
    psum x1 -> x0, waiting for transfers between devices: 119 us -> none  [local(): lax.psum(partial_sum.astype(jnp.bfloat16), 'tensor').astype(jnp.float32)]
    reduce_sum x0 -> x1, other arithmetic: none -> 23.8 us  [local(): jnp.sum(lax.all_gather(partial_sum.astype(jnp.bfloat16), 'tensor'), axis=0)]
    all_gather x1, waiting for transfers between devices: 87.7 us -> 65.8 us  [local(): resid_all = lax.all_gather(residual, 'tensor', axis=0, tiled=True)]
  transfers between devices with their start and end apart: 5 -> 5, of which waited for: 5 -> 5; matrix products, arithmetic and copies ran while one was open for 2% -> 3% of each run, Pallas kernels for 0% -> 0%
where the time goes in v1:
time: 1310 us
  waiting for transfers between devices  1060 us (81%)
  blocking collectives  169 us (13%)
  other arithmetic  35.6 us (3%)
  matrix products  27.2 us (2%)
  between operations  15.9 us (1%)
    all_gather x1, waiting for transfers between devices, local(): lax.all_gather(partial_sum.astype(jnp.bfloat16), 'tensor')  629 us
    reduce_scatter x1, waiting for transfers between devices, local(): lax.psum_scatter(lax.dot_general(columns, d_pre, contract, preferred_elem...  144 us
    unnamed x6, waiting for transfers between devices  115 us
    all_gather x1, waiting for transfers between devices, local(): lax.all_gather(twist_in, 'dp', axis=0, tiled=True)  105 us
    all_gather x3, blocking collectives, merged_2(): pieces = jax.tree.map(lambda part: lax.all_gather(part, axis), value)  81.4 us
    all_gather x1, waiting for transfers between devices, local(): resid_all = lax.all_gather(residual, 'tensor', axis=0, tiled=True)  65.8 us
    psum x1, blocking collectives, local(): lax.psum(jnp.dot(weights, active, precision=lax.Precision.HIGHEST), 'dp')  49.3 us
    psum x1, blocking collectives, local(): twist_vals = lax.psum(partial_psi, 'tensor') + token_bias[token_ids]  38.4 us
  transfers between devices with their start and end apart: 5, of which 5 were waited for; matrix products, arithmetic and copies ran while one was open for 3% of the time, Pallas kernels for 0%

profile of v1, /device:TPU:2, one launch (start us, length us, event | category | flops | bytes accessed | tf_op | source)
XLA Modules:
  0.0 1310.0 jit_solution(17498837386184655108)
XLA Ops:
  7.2 0.0 copy-start
  7.2 0.0 copy-start.4
  7.2 0.0 all-gather.13.cloned.1.call-start
  7.2 7.9 convolution_convert_fusion.1
  15.1 0.0 all-gather.13.cloned.1.call-update
  15.1 0.0 all-gather.9.cloned.1.call-start
  15.2 0.7 all-gather.9.cloned.1.call-update
  15.9 0.0 all-gather.11.cloned.1.call-start
  15.9 0.7 all-gather.11.cloned.1.call-update
  16.6 0.0 all-reduce.3.cloned.1.call-start
  18.0 33.4 %all-gather.4 = f32[16,1,256]{2,1,0:T(1,128)S(1)} all-gather(f32[1,1,256]{2,1,0:T(1,128)S(1)} %fusion.13), channel_id=1, replica_groups=mesh['dp'=16,'tensor'=16] {'dp'}, dimensions={0}, use_global_device_ids=true | all-gather | bytes 17408 | tf_op jit(solution)/shard_map/all_gather | solution.py:8
  51.4 24.1 %all-gather.3 = f32[16,1,256]{2,1,0:T(1,128)S(1)} all-gather(f32[1,1,256]{2,1,0:T(1,128)S(1)} %fusion.14), channel_id=1, replica_groups=mesh['dp'=16,'tensor'=16] {'dp'}, dimensions={0}, use_global_device_ids=true | all-gather | bytes 17408 | tf_op jit(solution)/shard_map/all_gather | solution.py:8
  75.6 0.0 copy-done.4
  75.6 0.0 copy-done
  75.6 1.7 gather_fusion
  77.3 628.9 %all-gather.13.cloned.1.call-done = bf16[4096,8192]{1,0:T(8,128)(2,1)} async-done(((bf16[256,8192]{1,0:T(8,128)(2,1)}), bf16[4096,8192]{1,0:T(8,128)(2,1)}) %all-gather.13.cloned.1.call-update) | async-done | bytes 67108880 | tf_op jit(solution)/shard_map/all_gather | solution.py:44
  706.2 23.8 %reduce_sum.21 = bf16[256,8192]{1,0:T(8,128)(2,1)} reduce(bf16[16,256,8192]{2,1,0:T(8,128)(2,1)} %bitcast.3, bf16[]{:T(256)} %constant.9.clone.1), dimensions={0}, to_apply=%region_0.0 | reduce | flops 31457280 | bytes 71303168 | tf_op jit(solution)/shard_map/reduce_sum | solution.py:44
  730.1 0.0 copy-done.1
  730.1 0.0 copy-done.2
  730.1 65.8 %all-gather.9.cloned.1.call-done = bf16[256,8192]{1,0:T(8,128)(2,1)} async-done(((bf16[16,8192]{1,0:T(8,128)(2,1)}), bf16[256,8192]{1,0:T(8,128)(2,1)}) %all-gather.9.cloned.1.call-update) | async-done | bytes 4194320 | tf_op jit(solution)/shard_map/all_gather | solution.py:47
  795.8 4.9 fusion
  800.8 0.0 slice-start
  800.8 0.0 slice-start.1
  800.8 104.6 %all-gather.11.cloned.1.call-done = bf16[8192,512]{1,0:T(8,128)(2,1)} async-done(((bf16[512,512]{1,0:T(8,128)(2,1)}), bf16[8192,512]{1,0:T(8,128)(2,1)}) %all-gather.11.cloned.1.call-update) | async-done | bytes 8388624 | tf_op jit(solution)/shard_map/all_gather | solution.py:53
  905.4 0.0 copy-done.5
  905.4 8.2 fusion.20
  913.6 0.0 copy-done.6
  913.6 0.6 fusion.11
  914.2 38.4 %psum.14 = f32[256]{0:T(256)S(1)} all-reduce(f32[256]{0:T(256)S(1)} %bitcast.54), channel_id=1, replica_groups=mesh['dp'=16,'tensor'=16] {'tensor'}, use_global_device_ids=true, to_apply=%region_2.3 | all-reduce | flops 256 | bytes 2048 | tf_op jit(solution)/shard_map/psum | solution.py:58
  952.6 23.8 %all-gather.2 = f32[16,1,256]{2,1,0:T(1,128)S(1)} all-gather(f32[1,1,256]{2,1,0:T(1,128)S(1)} %bitcast.52), channel_id=3, replica_groups=mesh['dp'=16,'tensor'=16] {'dp'}, dimensions={0}, use_global_device_ids=true | all-gather | bytes 17408 | tf_op jit(solution)/shard_map/all_gather | solution.py:8
  976.4 0.0 slice-done
  976.4 0.0 slice-done.1
  976.4 1.3 while.14
  977.7 2.1 scatter_custom_fusion
  979.8 0.7 convert_element_type.63
  980.5 0.0 all-reduce.3.cloned.1.call-update
  980.6 0.2 reduce-scatter.2.cloned.1.call-start
  980.8 10.1 convolution_convert_fusion
  990.9 0.0 copy-done.3
  990.9 0.0 reduce-scatter.2.cloned.1.call-update
  990.9 0.6 copy-done.7
  991.5 0.6 dynamic-slice
  992.8 0.5 fusion.9
  993.2 49.3 %psum.15 = f32[512]{0:T(512)} all-reduce(f32[512]{0:T(512)S(1)} %bitcast.53), channel_id=1, replica_groups=mesh['dp'=16,'tensor'=16] {'dp'}, use_global_device_ids=true, to_apply=%region_6.7 | all-reduce | flops 512 | bytes 4096 | tf_op jit(solution)/shard_map/psum | solution.py:66
  1042.5 113.2 %all-reduce.3.cloned.1.call-done = bf16[128256]{0:T(1024)(128)(2,1)} async-done(((bf16[128256]{0:T(1024)(128)(2,1)}), bf16[128256]{0:T(1024)(128)(2,1)}) %all-reduce.3.cloned.1.call-update) | async-done | bytes 256528
  1155.7 1.4 dynamic-slice_convert_fusion
  1157.1 144.2 %reduce-scatter.2.cloned.1.call-done = bf16[512,512]{1,0:T(8,128)(2,1)} async-done(((bf16[8192,512]{1,0:T(8,128)(2,1)}), bf16[512,512]{1,0:T(8,128)(2,1)}) %reduce-scatter.2.cloned.1.call-update) | async-done | bytes 524304 | tf_op jit(solution)/shard_map/reduce_scatter | solution.py:77
  1301.3 2.1 convert_element_type.62
  (80 shorter events, 0.9 us)
Async XLA Ops:
  7.2 68.4 %copy-start = (f32[128256]{0:T(1024)S(1)}, f32[128256]{0:T(1024)}, u32[]{:S(2)}) copy-start(f32[128256]{0:T(1024)} %param.19) | copy-start | bytes 1539076
  7.2 68.4 %copy-start.4 = (s32[256]{0:T(256)S(1)}, s32[256]{0:T(256)}, u32[]{:S(2)}) copy-start(s32[256]{0:T(256)} %param.12) | copy-start | bytes 3076
  7.2 699.0 %all-gather.13.cloned.1.call-start = ((), (), s32[]{:S(2)}) async-start(), calls=%async_computation.4 | async-start | bytes 71303168 | tf_op jit(solution)/shard_map/all_gather | solution.py:44
  15.1 780.7 %all-gather.9.cloned.1.call-start = ((), (), s32[]{:S(2)}) async-start(), calls=%async_computation.1 | async-start | bytes 4456448 | tf_op jit(solution)/shard_map/all_gather | solution.py:47
  15.9 889.5 %all-gather.11.cloned.1.call-start = ((), (), s32[]{:S(2)}) async-start(), calls=%async_computation.2 | async-start | bytes 8912896 | tf_op jit(solution)/shard_map/all_gather | solution.py:53
  16.6 1139.1 %all-reduce.3.cloned.1.call-start = ((), (), s32[]{:S(2)}) async-start(), calls=%async_computation.5 | async-start | bytes 516096
  51.4 678.7 %copy-start.1 = (f32[16,1,256]{2,1,0:T(1,128)}, f32[16,1,256]{2,1,0:T(1,128)S(1)}, u32[]{:S(2)}) copy-start(f32[16,1,256]{2,1,0:T(1,128)S(1)} %all-gather.4) | copy-start | bytes 49156
  75.5 654.5 %copy-start.2 = (f32[16,1,256]{2,1,0:T(1,128)}, f32[16,1,256]{2,1,0:T(1,128)S(1)}, u32[]{:S(2)}) copy-start(f32[16,1,256]{2,1,0:T(1,128)S(1)} %all-gather.3) | copy-start | bytes 49156
  730.1 175.3 %copy-start.5 = (f32[8192]{0:T(1024)S(1)}, f32[8192]{0:T(1024)}, u32[]{:S(2)}) copy-start(f32[8192]{0:T(1024)} %param.16) | copy-start | bytes 98308
  800.8 112.9 %copy-start.6 = (f32[512]{0:T(512)S(1)}, f32[512]{0:T(512)}, u32[]{:S(2)}) copy-start(f32[512]{0:T(512)} %param.18) | copy-start | bytes 6148
  800.8 175.7 %slice-start = ((f32[16,1,256]{2,1,0:T(1,128)}), f32[1,1,256]{2,1,0:T(1,128)S(1)}, s32[]{:S(2)}) async-start(f32[16,1,256]{2,1,0:T(1,128)} %copy-done.1), calls=%async_computation.6 | async-start | bytes 2048 | tf_op jit(solution)/shard_map/slice | solution.py:9
  800.8 175.6 %slice-start.1 = ((f32[16,1,256]{2,1,0:T(1,128)}), f32[1,1,256]{2,1,0:T(1,128)S(1)}, s32[]{:S(2)}) async-start(f32[16,1,256]{2,1,0:T(1,128)} %copy-done.2), calls=%async_computation.7 | async-start | bytes 2048 | tf_op jit(solution)/shard_map/slice | solution.py:9
  952.6 38.3 %copy-start.3 = (f32[256]{0:T(256)}, f32[256]{0:T(256)S(1)}, u32[]{:S(2)}) copy-start(f32[256]{0:T(256)S(1)} %get-tuple-element.63) | copy-start | bytes 3076
  980.6 320.8 %reduce-scatter.2.cloned.1.call-start = ((), (), s32[]{:S(2)}) async-start(), calls=%async_computation.3 | async-start | bytes 8912896 | tf_op jit(solution)/shard_map/reduce_scatter | solution.py:77
  990.9 0.7 copy-start.7
Sparse Core Ops, SparseCore 0:
  15.3 690.9 all-gather.12
  708.0 87.7 all-gather.8
  798.5 106.8 all-gather.10
  980.7 174.9 all-reduce.2
  1160.2 141.1 reduce-scatter.1
